TPU v7x, 512 devices: a whole 4x4x16 slice. The times are simulated.
512 devices in a mesh: req: 128 (over z, y, core), wt: 4 (over x).
Axes of the slice: x: 4, y: 4, z: 16, core: 2. Of those that a mesh axis runs over, the one named last changes fastest.
Arguments:
- hidden_in: bfloat16 [32768, 5120], P('req', 'wt'), may hold values from -6 to 6
- queries: bfloat16 [32768, 5120], P('req', 'wt'), as said below
- key_proj: bfloat16 [32768, 5120], P('req', 'wt'), as said below
- values: bfloat16 [32768, 5120], P('req', 'wt'), may hold values from -6 to 6
- query_gain: float32 [5120], P('wt'), may hold values from 0.1 to 1.9
- key_gain: float32 [5120], P('wt'), may hold values from 0.1 to 1.9
- attn_gain: float32 [5120], P('wt'), may hold values from 0.1 to 1.9
- gate_w: bfloat16 [5120, 13824], P('wt', 'req'), may hold values from -0.078125 to 0.078125
- up_w: bfloat16 [5120, 13824], P('wt', 'req'), may hold values from -0.078125 to 0.078125
- lengths: int32 [128], replicated, may hold values from 1 to 256, 4608 in all
- assign: int32 [128], replicated, may hold values from 0 to 127, each once
- page_table: int32 [128, 2], P('req'), may hold values from 0 to 1, each once within a row
Outputs:
- gated: bfloat16 [128, 36, 13824], P(None, 'wt', 'req')
- key_cache: bfloat16 [256, 128, 5120], P('req', None, 'wt')
- value_cache: bfloat16 [256, 128, 5120], P('req', None, 'wt')
Inputs may be any that keep to these rules, and one draw needn't show every extreme that they name: lengths sum to 4608 and at least one request has exactly 256 tokens. `assign`: each device of req serves exactly one request. `page_table`: each row names each of the 2 pages of one device once. `queries`: real-valued entries within -24 to 24. `key_proj`: real-valued entries within -24 to 24.
All inputs are finite; a program needn't handle non-finite values.
Results may differ from a plain program's by a relative error of at most 0.013.
Values may be sent and summed in bfloat16 or wider, within the bound.
No kernel may reach another device: no remote copies, remote signals or barrier semaphores. Data moves between devices by JAX's collectives and lax.ppermute only.
A program may use at most 128 MiB of HBM per device.

v0:
```python
import jax
import jax.numpy as jnp
from jax import lax
from jax.sharding import PartitionSpec as P

D = 5120
HD = 128
PAGE = 128
LIVE = 36
EPS = 1e-06
THETA = 500000.0


def rope_tables(row_count, head_width):
    half_width = head_width // 2
    frequency = THETA ** (-(jnp.arange(half_width, dtype=jnp.float32) * 2.0 / head_width))
    angles = jnp.arange(row_count, dtype=jnp.float32)[:, None] * frequency[None, :]
    return (jnp.cos(angles), jnp.sin(angles))


def rotate(heads_in, cosine, sine_table):
    half_width = heads_in.shape[-1] // 2
    leading = heads_in[..., :half_width]
    trailing = heads_in[..., half_width:]
    cos_b = cosine[:, None, :]
    sin_b = sine_table[:, None, :]
    return jnp.concatenate(
        [leading * cos_b - trailing * sin_b, trailing * cos_b + leading * sin_b], axis=-1
    )


def deal_rows(source, owner_start, owner_len, device, owners, live_rows):
    slot_count = source.shape[0]
    feature_count = source.shape[1]
    per_peer = slot_count // owners
    column = jnp.arange(per_peer, dtype=jnp.int32)[None, :]
    target_dev = jnp.arange(owners, dtype=jnp.int32)[:, None]
    my_start = owner_start[device]
    my_length = owner_len[device]
    local_index = (target_dev - my_start) % owners + owners * column
    usable = local_index < my_length
    picked = jnp.where(
        usable[:, :, None],
        source[jnp.minimum(local_index, slot_count - 1)],
        jnp.zeros((), source.dtype),
    )
    arrived = lax.all_to_all(picked, "req", split_axis=0, concat_axis=0, tiled=True)
    src_start = owner_start[:, None]
    src_length = owner_len[:, None]
    sent_index = (device - src_start) % owners + owners * column
    landing = jnp.where(
        sent_index < src_length, (src_start + sent_index - device) // owners, live_rows
    )
    packed = jnp.zeros((live_rows, feature_count), source.dtype)
    return packed.at[landing.reshape(-1)].set(arrived.reshape(-1, feature_count), mode="drop")


def per_device(
    hidden_in,
    queries,
    key_proj,
    values,
    query_gain,
    key_gain,
    attn_gain,
    gate_w,
    up_w,
    lengths,
    assign,
    page_table,
):
    slot_count = hidden_in.shape[0]
    feature_count = hidden_in.shape[1]
    owners = lax.axis_size("req")
    device = lax.axis_index("req")
    head_count = feature_count // HD
    unit_count = gate_w.shape[1]
    owner_req = jnp.zeros((owners,), jnp.int32).at[assign].set(jnp.arange(owners, dtype=jnp.int32))
    starts = jnp.cumsum(lengths) - lengths
    owner_start = starts[owner_req]
    owner_len = lengths[owner_req]
    my_length = owner_len[device]
    query_f = queries.astype(jnp.float32)
    key_f = key_proj.astype(jnp.float32)
    query_sq, key_sq = lax.psum(
        (jnp.sum(query_f * query_f, axis=1), jnp.sum(key_f * key_f, axis=1)), "wt"
    )
    query_n = query_f * lax.rsqrt(query_sq / D + EPS)[:, None] * query_gain
    key_n = key_f * lax.rsqrt(key_sq / D + EPS)[:, None] * key_gain
    cosine, sine_table = rope_tables(slot_count, HD)
    query_r = rotate(query_n.reshape(slot_count, head_count, HD), cosine, sine_table).astype(
        jnp.bfloat16
    )
    key_r = rotate(key_n.reshape(slot_count, head_count, HD), cosine, sine_table).astype(
        jnp.bfloat16
    )
    scores = jnp.einsum(
        "qhd,khd->hqk", query_r, key_r, preferred_element_type=jnp.float32
    ) * HD ** (-0.5)
    position = jnp.arange(slot_count, dtype=jnp.int32)
    allowed = (position[None, :] <= position[:, None]) & (position[None, :] < my_length)
    scores = jnp.where(allowed[None], scores, -jnp.inf)
    row_peak = jnp.max(scores, axis=2, keepdims=True)
    expd = jnp.exp(scores - row_peak)
    probabilities = (expd / jnp.sum(expd, axis=2, keepdims=True)).astype(jnp.bfloat16)
    value_heads = values.reshape(slot_count, head_count, HD)
    attended = jnp.einsum(
        "hqk,khd->qhd", probabilities, value_heads, preferred_element_type=jnp.float32
    )
    attended = attended.astype(jnp.bfloat16).reshape(slot_count, feature_count)
    attended_f = attended.astype(jnp.float32)
    attn_sq = lax.psum(jnp.sum(attended_f * attended_f, axis=1), "wt")
    layer_rows = (
        hidden_in.astype(jnp.float32)
        + attended_f * lax.rsqrt(attn_sq / D + EPS)[:, None] * attn_gain
    ).astype(jnp.bfloat16)
    live_mask = (position < my_length)[:, None]
    page_count = slot_count // PAGE
    zero_value = jnp.zeros((), jnp.bfloat16)
    key_pages = jnp.where(live_mask, key_r.reshape(slot_count, feature_count), zero_value).reshape(
        page_count, PAGE, feature_count
    )
    value_pages = jnp.where(live_mask, values, zero_value).reshape(page_count, PAGE, feature_count)
    placement = page_table[0]
    key_cache = jnp.zeros_like(key_pages).at[placement].set(key_pages)
    value_cache = jnp.zeros_like(value_pages).at[placement].set(value_pages)
    regrouped = deal_rows(layer_rows, owner_start, owner_len, device, owners, LIVE)
    piece = lax.all_gather(regrouped, "req", axis=0, tiled=True)
    stacked = jnp.stack(
        [
            jnp.dot(piece, gate_w, preferred_element_type=jnp.float32),
            jnp.dot(piece, up_w, preferred_element_type=jnp.float32),
        ]
    )
    stacked = stacked.reshape(2, owners, LIVE, unit_count)
    gate_part, up_part = (
        lax.psum_scatter(stacked[0], "wt", scatter_dimension=1, tiled=True),
        lax.psum_scatter(stacked[1], "wt", scatter_dimension=1, tiled=True),
    )
    gated = (jax.nn.silu(gate_part) * up_part).astype(jnp.bfloat16)
    return (gated, key_cache, value_cache)


def solution(mesh):
    placed = (
        P("req", "wt"),
        P("req", "wt"),
        P("req", "wt"),
        P("req", "wt"),
        P("wt"),
        P("wt"),
        P("wt"),
        P("wt", "req"),
        P("wt", "req"),
        P(),
        P(),
        P("req", None),
    )
    return jax.shard_map(
        per_device,
        mesh=mesh,
        in_specs=placed,
        out_specs=(P(None, "wt", "req"), P("req", None, "wt"), P("req", None, "wt")),
        check_vma=False,
    )
```

profile of v0, /device:TPU:1, one launch (start us, length us, event | category | flops | bytes accessed | tf_op | source)
XLA Modules:
  0.0 378.9 jit_solution(4246838663136592697)
XLA Ops:
  7.2 1.4 copy.56
  8.6 0.2 fusion.3
  8.8 0.2 copy.59
  9.1 0.2 fusion.5
  9.3 9.3 %all-reduce = (f32[256]{0:T(256)S(1)}, f32[256]{0:T(256)S(1)}) all-reduce(f32[256]{0:T(256)S(1)} %fusion.5, f32[256]{0:T(256)S(1)} %fusion.3), channel_id=1, replica_groups=mesh['req'=128,'wt'=4] {'wt'}, use_global_device_ids=true, to_apply=%region_5.6 | all-reduce | flops 512 | bytes 4096 | tf_op jit(solution)/shard_map/psum | solution.py:85
  18.6 0.2 fusion.6
  18.8 1.0 fusion.37
  19.8 1.5 copy.78
  21.3 1.5 copy.79
  22.8 0.5 fusion.20
  23.3 0.2 fusion.4
  23.6 1.0 fusion.36
  24.5 1.5 copy.76
  26.0 2.6 copy.77
  28.6 1.0 scatter_custom_fusion
  29.7 1.2 gather_fusion.1
  30.9 0.6 dynamic_slice.8
  31.5 0.6 iota_compare_fusion.1
  32.2 1.1 copy.62
  33.2 1.9 multiply_subtract_fusion
  35.2 0.4 maximum_convert_fusion
  35.6 0.9 copy-done.3
  36.5 1.5 subtract_convert_fusion
  38.0 4.1 %fusion.38 = (f32[10,256]{1,0:T(8,128)S(1)}, f32[10,256,256]{1,2,0:T(8,128)}) fusion(pred[256,256]{0,1:T(8,128)(4,1)S(1)} %fusion.14, bf16[256,10,128]{2,0,1:T(8,128)(2,1)S(1)} %maximum_convert_fusion, bf16[256,10,64]{2,0,1:T(8,128)(2,1)} %get-tuple-element.9, bf16[256,10,64]{2,0,1:T(8,128)(2,1)} %get-tuple-element.8), kind=kOutput, calls=%fused_computation.86 | convolution fusion | flops 171704576 | bytes 4007936 | tf_op jit(solution)/shard_map/sub | solution.py:104
  42.0 3.2 multiply_reduce_fusion
  45.2 1.7 copy.64
  47.0 6.0 %psum.23 = f32[256]{0:T(256)S(1)} all-reduce(f32[256]{0:T(256)S(1)} %get-tuple-element.22), channel_id=1, replica_groups=mesh['req'=128,'wt'=4] {'wt'}, use_global_device_ids=true, to_apply=%region_9.10 | all-reduce | flops 256 | bytes 2048 | tf_op jit(solution)/shard_map/psum | solution.py:112
  53.1 0.2 reduce-window.9
  53.4 1.2 gather_fusion
  54.6 0.6 dynamic_slice.7
  55.2 0.7 and_select_fusion.1
  56.0 0.1 reshape.445
  56.1 1.4 add_convert_fusion
  57.5 1.2 gather_fusion.2
  58.8 0.2 reshape.444
  59.0 0.6 add_compare_fusion.2
  59.7 0.1 copy.55
  59.8 1.5 broadcast_select_fusion
  61.3 23.5 %all-to-all-start = ((bf16[128,2,1280]{2,1,0:T(2,128)(2,1)}), bf16[128,2,1280]{2,1,0:T(2,128)(2,1)S(1)}, u32[]{:S(2)}, u32[]{:S(2)}) async-start(bf16[128,2,1280]{2,1,0:T(2,128)(2,1)} %broadcast_select_fusion), calls=%async_computation | async-start | bytes 1310720 | tf_op jit(solution)/shard_map/all_to_all | solution.py:47
  84.9 0.1 copy.53
  85.0 0.1 lt.111
  85.3 0.1 sub.67
  85.5 35.7 %all-to-all-done = bf16[128,2,1280]{2,1,0:T(2,128)(2,1)S(1)} async-done(((bf16[128,2,1280]{2,1,0:T(2,128)(2,1)}), bf16[128,2,1280]{2,1,0:T(2,128)(2,1)S(1)}, u32[]{:S(2)}, u32[]{:S(2)}) %all-to-all-start) | async-done | bytes 655392 | tf_op jit(solution)/shard_map/all_to_all | solution.py:47
  121.2 0.2 reshape.463
  121.5 2.2 scatter_custom_fusion.1
  123.8 146.6 %all-gather.3.cloned.1.call-done = bf16[128,36,1280]{2,1,0:T(8,128)(2,1)} async-done(((bf16[1,36,1280]{2,1,0:T(8,128)(2,1)}), bf16[128,36,1280]{2,1,0:T(8,128)(2,1)}) %all-gather.3.cloned.1.call-update) | async-done | bytes 11796496 | tf_op jit(solution)/shard_map/all_gather | solution.py:128
  270.4 16.9 %reshape.488 = bf16[4608,1280]{1,0:T(8,128)(2,1)} reshape(bf16[128,36,1280]{2,1,0:T(8,128)(2,1)} %all-gather.3.cloned.1.call-done) | data formatting | bytes 23592960
  287.3 6.1 %fusion.41 = f32[4608,108]{1,0:T(8,128)S(1)} fusion(bf16[4608,1280]{1,0:T(8,128)(2,1)} %reshape.488, bf16[1280,108]{0,1:T(8,128)(2,1)S(1)} %copy-done), kind=kOutput, calls=%fused_computation.87 | convolution fusion | flops 1274019840 | bytes 14063616 | tf_op jit(solution)/shard_map/dot_general | solution.py:131
  293.4 1.6 squeeze.18
  295.0 3.3 copy.66
  298.4 0.9 copy-done.11
  299.3 6.1 %fusion.42 = f32[4608,108]{1,0:T(8,128)S(1)} fusion(bf16[4608,1280]{1,0:T(8,128)(2,1)} %reshape.488, bf16[1280,108]{0,1:T(8,128)(2,1)S(1)} %copy-done.11), kind=kOutput, calls=%fused_computation.88 | convolution fusion | flops 1274019840 | bytes 14063616 | tf_op jit(solution)/shard_map/dot_general | solution.py:132
  305.4 1.6 squeeze.19
  307.0 3.3 copy.68
  310.4 1.1 copy-done.8
  311.4 0.5 copy.74
  311.9 0.4 reshape.489
  312.3 0.6 add_compare_fusion.1
  313.0 0.9 broadcast.359.clone
  313.9 2.5 scatter_fusion
  316.6 0.7 scatter_fusion.1
  317.3 13.0 %reduce-scatter.3.cloned.1.call-done = f32[128,9,108]{0,2,1:T(8,128)} async-done(((f32[128,36,108]{0,2,1:T(8,128)}), f32[128,9,108]{0,2,1:T(8,128)}) %reduce-scatter.3.cloned.1.call-update) | async-done | bytes 497680 | tf_op jit(solution)/shard_map/reduce_scatter | solution.py:137
  330.3 40.0 %reduce-scatter.5.cloned.1.call-done = f32[128,9,108]{0,2,1:T(8,128)} async-done(((f32[128,36,108]{0,2,1:T(8,128)}), f32[128,9,108]{0,2,1:T(8,128)}) %reduce-scatter.5.cloned.1.call-update) | async-done | bytes 497680 | tf_op jit(solution)/shard_map/reduce_scatter | solution.py:138
  370.3 2.0 multiply_convert_fusion
  (58 shorter events, 1.2 us)
Async XLA Ops:
  7.2 280.1 %copy-start = (bf16[1280,108]{0,1:T(8,128)(2,1)S(1)}, bf16[1280,108]{0,1:T(8,128)(2,1)}, u32[]{:S(2)}) copy-start(bf16[1280,108]{0,1:T(8,128)(2,1)} %param.19) | copy-start | bytes 829444
  7.2 1.7 copy-start.9
  8.6 10.0 %copy-start.12 = (f32[1280]{0:T(1024)S(1)}, f32[1280]{0:T(1024)}, u32[]{:S(2)}) copy-start(f32[1280]{0:T(1024)} %param.17) | copy-start | bytes 15364
  21.3 2.0 copy-start.13
  26.0 2.7 copy-start.15
  26.0 3.7 copy-start.2
  26.0 6.2 %copy-start.5 = (bf16[256,1280]{1,0:T(8,128)(2,1)S(1)}, bf16[256,1280]{1,0:T(8,128)(2,1)}, u32[]{:S(2)}) copy-start(bf16[256,1280]{1,0:T(8,128)(2,1)} %param.15) | copy-start | bytes 1966084
  33.2 2.3 copy-start.4
  35.2 1.3 copy-start.3
  36.5 1.5 copy-start.7
  38.0 4.1 %copy-start.10 = (bf16[256,1280]{0,1:T(8,128)(2,1)S(1)}, bf16[256,1280]{0,1:T(8,128)(2,1)}, u32[]{:S(2)}) copy-start(bf16[256,1280]{0,1:T(8,128)(2,1)} %copy.62) | copy-start | bytes 1966084
  45.2 10.9 %copy-start.14 = (f32[1280]{0:T(1024)S(1)}, f32[1280]{0:T(1024)}, u32[]{:S(2)}) copy-start(f32[1280]{0:T(1024)} %param.18) | copy-start | bytes 15364
  61.3 59.9 %all-to-all-start = ((bf16[128,2,1280]{2,1,0:T(2,128)(2,1)}), bf16[128,2,1280]{2,1,0:T(2,128)(2,1)S(1)}, u32[]{:S(2)}, u32[]{:S(2)}) async-start(bf16[128,2,1280]{2,1,0:T(2,128)(2,1)} %broadcast_select_fusion), calls=%async_computation | async-start | bytes 1310720 | tf_op jit(solution)/shard_map/all_to_all | solution.py:47
  84.8 185.6 %all-gather.3.cloned.1.call-start = ((), (), s32[]{:S(2)}) async-start(), calls=%async_computation.5 | async-start | bytes 13209600 | tf_op jit(solution)/shard_map/all_gather | solution.py:128
  123.7 206.6 %reduce-scatter.3.cloned.1.call-start = ((), (), s32[]{:S(2)}) async-start(), calls=%async_computation.3 | async-start | bytes 2580480 | tf_op jit(solution)/shard_map/reduce_scatter | solution.py:137
  298.3 1.0 copy-start.11
  298.4 72.0 %reduce-scatter.5.cloned.1.call-start = ((), (), s32[]{:S(2)}) async-start(), calls=%async_computation.4 | async-start | bytes 2580480 | tf_op jit(solution)/shard_map/reduce_scatter | solution.py:138
  310.3 1.1 copy-start.8
  311.4 1.4 copy-start.16
  316.5 55.8 %copy-start.1 = (bf16[1280,108]{0,1:T(8,128)(2,1)S(1)}, bf16[1280,108]{0,1:T(8,128)(2,1)}, u32[]{:S(2)}) copy-start(bf16[1280,108]{0,1:T(8,128)(2,1)} %param.19) | copy-start | bytes 829444
  317.3 55.0 %copy-start.6 = (bf16[2,128,1280]{2,1,0:T(8,128)(2,1)}, bf16[2,128,1280]{2,1,0:T(8,128)(2,1)S(1)}, u32[]{:S(2)}) copy-start(bf16[2,128,1280]{2,1,0:T(8,128)(2,1)S(1)} %scatter_fusion.1) | copy-start | bytes 1966084
Sparse Core Ops, SparseCore 0:
  123.9 146.5 all-gather.2
  298.5 31.7 reduce-scatter.2
  333.4 36.8 reduce-scatter.4
where the time goes:
time: 380 us; the launch traced here: 379 us
  waiting for transfers between devices  235 us (62%)
  local copies, waits for them, and re-layouts  57.6 us (15%)
  starting transfers between devices  23.6 us (6%)
  matrix products  19.5 us (5%)
  blocking collectives  15.3 us (4%)
  between operations  14.1 us (4%)
  other arithmetic  13.3 us (4%)
    all_gather x1, waiting for transfers between devices, per_device(): piece = lax.all_gather(regrouped, 'req', axis=0, tiled=True)  147 us
    reduce_scatter x1, waiting for transfers between devices, per_device(): lax.psum_scatter(stacked[1], 'wt', scatter_dimension=1, tiled=True)  40 us
    all_to_all x1, waiting for transfers between devices, deal_rows(): lax.all_to_all(picked, 'req', split_axis=0, concat_axis=0, tiled=True)  35.7 us
    unnamed x42, local copies, waits for them, and re-layouts  29.6 us
    all_to_all x1, starting transfers between devices, deal_rows(): lax.all_to_all(picked, 'req', split_axis=0, concat_axis=0, tiled=True)  23.5 us
    reduce_scatter x1, waiting for transfers between devices, per_device(): lax.psum_scatter(stacked[0], 'wt', scatter_dimension=1, tiled=True)  13 us
    psum x1, blocking collectives, per_device(): lax.psum((jnp.sum(query_f * query_f, axis=1), jnp.sum(key_f * key_f, axis...  9.29 us
  transfers between devices with their start and end apart: 4, of which 4 were waited for; matrix products, arithmetic and copies ran while one was open for 5% of the time, Pallas kernels for 0%

commit v1 on v0

--- a/solution.py
+++ b/solution.py
@@ -125,7 +125,9 @@
     key_cache = jnp.zeros_like(key_pages).at[placement].set(key_pages)
     value_cache = jnp.zeros_like(value_pages).at[placement].set(value_pages)
     regrouped = deal_rows(layer_rows, owner_start, owner_len, device, owners, LIVE)
-    piece = lax.all_gather(regrouped, "req", axis=0, tiled=True)
+    piece = jnp.concatenate(
+        lax.all_to_all(jnp.stack([regrouped] * lax.axis_size("req")), "req", 0, 0), axis=0
+    )
     stacked = jnp.stack(
         [
             jnp.dot(piece, gate_w, preferred_element_type=jnp.float32),

time: 380 us -> 793 us (2.09)
  blocking collectives: 15.3 us -> 595 us
  waiting for transfers between devices: 235 us -> 90.8 us
  local copies, waits for them, and re-layouts: 57.6 us -> 36 us
    all_to_all x0 -> x1, blocking collectives: none -> 580 us  [per_device(): lax.all_to_all(jnp.stack([regrouped] * lax.axis_size('req')), 'req', 0, 0)]
    all_gather x1 -> x0, waiting for transfers between devices: 147 us -> none  [per_device(): piece = lax.all_gather(regrouped, 'req', axis=0, tiled=True)]
    unnamed x42 -> x41, local copies, waits for them, and re-layouts: 29.6 us -> 16.5 us
    squeeze x4 -> x0, local copies, waits for them, and re-layouts: 9.86 us -> none  [the longest x2 4.94 us: per_device(): stacked[1]]
  transfers between devices with their start and end apart: 4 -> 3, of which waited for: 4 -> 3; matrix products, arithmetic and copies ran while one was open for 5% -> 2% of each run, Pallas kernels for 0% -> 0%
where the time goes in v1:
time: 793 us; the launch traced here: 792 us
  blocking collectives  595 us (75%)
  waiting for transfers between devices  90.8 us (11%)
  local copies, waits for them, and re-layouts  36 us (5%)
  starting transfers between devices  23.8 us (3%)
  matrix products  21.5 us (3%)
  between operations  14.5 us (2%)
  other arithmetic  10.9 us (1%)
    all_to_all x1, blocking collectives, per_device(): lax.all_to_all(jnp.stack([regrouped] * lax.axis_size('req')), 'req', 0, 0)  580 us
    reduce_scatter x1, waiting for transfers between devices, per_device(): lax.psum_scatter(stacked[1], 'wt', scatter_dimension=1, tiled=True)  40 us
    all_to_all x1, waiting for transfers between devices, deal_rows(): lax.all_to_all(picked, 'req', split_axis=0, concat_axis=0, tiled=True)  35.7 us
    all_to_all x1, starting transfers between devices, deal_rows(): lax.all_to_all(picked, 'req', split_axis=0, concat_axis=0, tiled=True)  23.5 us
    unnamed x41, local copies, waits for them, and re-layouts  16.5 us
  transfers between devices with their start and end apart: 3, of which 3 were waited for; matrix products, arithmetic and copies ran while one was open for 2% of the time, Pallas kernels for 0%

profile of v1, /device:TPU:1, one launch (start us, length us, event | category | flops | bytes accessed | tf_op | source)
XLA Modules:
  0.0 792.4 jit_solution(4387744597601103627)
XLA Ops:
  7.2 1.4 copy.49
  8.6 0.2 fusion.7
  8.8 0.2 copy.52
  9.1 0.2 fusion.9
  9.3 9.3 %all-reduce = (f32[256]{0:T(256)S(1)}, f32[256]{0:T(256)S(1)}) all-reduce(f32[256]{0:T(256)S(1)} %fusion.9, f32[256]{0:T(256)S(1)} %fusion.7), channel_id=1, replica_groups=mesh['req'=128,'wt'=4] {'wt'}, use_global_device_ids=true, to_apply=%region_5.6 | all-reduce | flops 512 | bytes 4096 | tf_op jit(solution)/shard_map/psum | solution.py:85
  18.6 0.2 fusion.10
  18.8 0.9 fusion.43
  19.8 1.5 copy.67
  21.3 1.5 copy.68
  22.8 0.5 fusion.26
  23.3 0.2 fusion.8
  23.6 1.5 copy.65
  25.1 1.5 copy.66
  26.6 1.0 scatter_custom_fusion
  27.6 1.2 gather_fusion.1
  28.9 0.6 dynamic_slice.8
  29.4 0.6 iota_compare_fusion.1
  30.2 2.2 copy.55
  32.4 0.4 multiply_subtract_fusion
  32.8 0.4 maximum_convert_fusion
  33.1 0.6 copy-done.5
  33.7 0.5 copy-done.4
  34.2 0.4 subtract_convert_fusion
  34.6 2.7 fusion.44
  37.3 3.2 multiply_reduce_fusion
  40.5 1.7 copy.57
  42.3 6.0 psum.23
  48.3 0.1 copy.45
  48.4 0.2 reduce-window.9
  48.7 1.2 gather_fusion
  49.9 0.6 dynamic_slice.7
  50.5 0.7 and_select_fusion.1
  51.3 0.1 reshape.452
  51.4 1.4 add_convert_fusion
  52.8 1.3 gather_fusion.2
  54.0 0.2 reshape.451
  54.3 0.7 add_compare_fusion.2
  55.0 0.1 copy.48
  55.2 1.5 broadcast_select_fusion
  56.7 23.5 %all-to-all-start = ((bf16[128,2,1280]{2,1,0:T(2,128)(2,1)}), bf16[128,2,1280]{2,1,0:T(2,128)(2,1)S(1)}, u32[]{:S(2)}, u32[]{:S(2)}) async-start(bf16[128,2,1280]{2,1,0:T(2,128)(2,1)} %broadcast_select_fusion), calls=%async_computation | async-start | bytes 1310720 | tf_op jit(solution)/shard_map/all_to_all | solution.py:47
  80.2 0.1 copy.46
  80.4 0.1 lt.111
  80.6 0.1 copy.47
  80.7 0.1 sub.67
  80.9 35.7 %all-to-all-done = bf16[128,2,1280]{2,1,0:T(2,128)(2,1)S(1)} async-done(((bf16[128,2,1280]{2,1,0:T(2,128)(2,1)}), bf16[128,2,1280]{2,1,0:T(2,128)(2,1)S(1)}, u32[]{:S(2)}, u32[]{:S(2)}) %all-to-all-start) | async-done | bytes 655392 | tf_op jit(solution)/shard_map/all_to_all | solution.py:47
  116.6 0.2 reshape.470
  116.9 1.6 scatter_custom_fusion.1
  118.5 5.5 stack.2
  124.0 579.6 %all_to_all.10 = bf16[128,36,1280]{2,1,0:T(8,128)(2,1)S(1)} all-to-all(bf16[128,36,1280]{2,1,0:T(8,128)(2,1)} %stack.2), channel_id=1, replica_groups=mesh['req'=128,'wt'=4] {'req'}, dimensions={0} | all-to-all | bytes 23592960 | tf_op jit(solution)/shard_map/all_to_all | solution.py:129
  703.5 4.7 copy-done.2
  708.2 5.4 fusion.3
  713.6 0.3 reduce-scatter.5.cloned.1.call-start
  713.9 0.7 copy-done.14
  714.6 10.2 %fusion.1 = f32[128,36,108]{0,2,1:T(8,128)} fusion(bf16[128,36,1280]{2,1,0:T(8,128)(2,1)} %copy-done.2, bf16[1280,108]{0,1:T(8,128)(2,1)S(1)} %copy-done.14), kind=kOutput, calls=%fused_computation.8 | convolution fusion | flops 1274019840 | bytes 14063616 | tf_op jit(solution)/shard_map/dot_general | solution.py:134
  724.8 0.5 copy.63
  725.2 0.4 reshape.496
  725.6 0.7 add_compare_fusion.1
  726.3 0.1 broadcast_select_fusion.2
  726.5 0.7 scatter_fusion
  727.2 0.3 copy-done.6
  727.7 0.7 scatter_fusion.1
  728.5 15.0 %reduce-scatter.3.cloned.1.call-done = f32[128,9,108]{0,2,1:T(8,128)} async-done(((f32[128,36,108]{0,2,1:T(8,128)}), f32[128,9,108]{0,2,1:T(8,128)}) %reduce-scatter.3.cloned.1.call-update) | async-done | bytes 497680 | tf_op jit(solution)/shard_map/reduce_scatter | solution.py:139
  743.5 40.0 %reduce-scatter.5.cloned.1.call-done = f32[128,9,108]{0,2,1:T(8,128)} async-done(((f32[128,36,108]{0,2,1:T(8,128)}), f32[128,9,108]{0,2,1:T(8,128)}) %reduce-scatter.5.cloned.1.call-update) | async-done | bytes 497680 | tf_op jit(solution)/shard_map/reduce_scatter | solution.py:140
  783.5 2.0 multiply_convert_fusion
  (52 shorter events, 0.9 us)
Async XLA Ops:
  7.2 701.0 %copy-start = (bf16[1280,108]{0,1:T(8,128)(2,1)S(1)}, bf16[1280,108]{0,1:T(8,128)(2,1)}, u32[]{:S(2)}) copy-start(bf16[1280,108]{0,1:T(8,128)(2,1)} %param.19) | copy-start | bytes 829444
  7.2 1.7 copy-start.9
  8.6 10.0 %copy-start.11 = (f32[1280]{0:T(1024)S(1)}, f32[1280]{0:T(1024)}, u32[]{:S(2)}) copy-start(f32[1280]{0:T(1024)} %param.17) | copy-start | bytes 15364
  21.3 2.0 copy-start.12
  25.1 1.5 copy-start.15
  25.1 2.5 copy-start.1
  26.6 5.8 copy-start.3
  32.4 1.3 copy-start.5
  32.7 1.4 copy-start.4
  34.6 2.7 copy-start.10
  40.5 10.9 %copy-start.13 = (f32[1280]{0:T(1024)S(1)}, f32[1280]{0:T(1024)}, u32[]{:S(2)}) copy-start(f32[1280]{0:T(1024)} %param.18) | copy-start | bytes 15364
  56.7 59.9 %all-to-all-start = ((bf16[128,2,1280]{2,1,0:T(2,128)(2,1)}), bf16[128,2,1280]{2,1,0:T(2,128)(2,1)S(1)}, u32[]{:S(2)}, u32[]{:S(2)}) async-start(bf16[128,2,1280]{2,1,0:T(2,128)(2,1)} %broadcast_select_fusion), calls=%async_computation | async-start | bytes 1310720 | tf_op jit(solution)/shard_map/all_to_all | solution.py:47
  80.2 663.3 %reduce-scatter.3.cloned.1.call-start = ((), (), s32[]{:S(2)}) async-start(), calls=%async_computation.4 | async-start | bytes 2580480 | tf_op jit(solution)/shard_map/reduce_scatter | solution.py:139
  703.5 4.7 copy-start.2
  713.6 1.0 copy-start.14
  713.6 69.9 %reduce-scatter.5.cloned.1.call-start = ((), (), s32[]{:S(2)}) async-start(), calls=%async_computation.5 | async-start | bytes 2580480 | tf_op jit(solution)/shard_map/reduce_scatter | solution.py:140
  724.7 1.6 copy-start.16
  726.4 1.1 copy-start.6
  727.5 0.9 copy-start.8
  728.5 57.1 %copy-start.7 = (bf16[2,128,1280]{2,1,0:T(8,128)(2,1)}, bf16[2,128,1280]{2,1,0:T(8,128)(2,1)S(1)}, u32[]{:S(2)}) copy-start(bf16[2,128,1280]{2,1,0:T(8,128)(2,1)S(1)} %scatter_fusion.1) | copy-start | bytes 1966084
Sparse Core Ops, SparseCore 0:
  713.8 29.6 reduce-scatter.2
  746.6 36.8 reduce-scatter.4
